TPU v7x, 512 devices: a whole 4x4x16 slice. The times are simulated.
512 devices in a mesh: src: 16 (over z_hi, x), dst: 32 (over z_lo, y, core).
Axes of the slice: x: 4, y: 4, z: 16 (z_hi: 4, z_lo: 4; z = z_hi * 4 + z_lo), core: 2. Of those that a mesh axis runs over, the one named last changes fastest.
Arguments:
- rel_ops: bfloat16 [2048, 400, 400], P(('src', 'dst')), may hold values from -0.3125 to 0.3125
- src_emb: bfloat16 [4096, 400], P('src'), may hold values from -1.796875 to 1.796875
- dst_emb: bfloat16 [8192, 400], P('dst'), may hold values from -6 to 6
- edge_src: int32 [16, 32, 1024], P('src', 'dst'), may hold values from 0 to 255
- edge_dst: int32 [16, 32, 1024], P('src', 'dst'), may hold values from 0 to 255
- slot_count: int32 [16, 32, 64], P('src', 'dst'), may hold values from 0 to 16
- neg_span: int32 [16, 2], P('src'), may hold values from 0 to 31
Outputs:
- grad_rel: bfloat16 [2048, 400, 400], P(('src', 'dst'))
- grad_src: bfloat16 [4096, 400], P('src')
- grad_dst: bfloat16 [8192, 400], P('dst')
All inputs are finite; a program needn't handle non-finite values.
Results may differ from a plain program's by a relative error of at most 0.015.
Values may be sent and summed in bfloat16 or wider, within the bound.
No kernel may reach another device: no remote copies, remote signals or barrier semaphores. Data moves between devices by JAX's collectives and lax.ppermute only.
A program may use at most 64 MiB of HBM per device.

v0:
```python
import jax
import jax.numpy as jnp
from jax import lax
from jax.sharding import PartitionSpec as P


def from_root(block, axis, holder):
    block = jnp.where(lax.axis_index(axis) == holder, block, jnp.zeros_like(block))
    return lax.psum(block, axis)


def send_back(rows_out):
    return lax.all_to_all(rows_out, "src", split_axis=0, concat_axis=0, tiled=True)


def body(rel_ops, src_emb, dst_emb, edge_src, edge_dst, slot_count, neg_span):
    n_src = lax.axis_size("src")
    rel_count = rel_ops.shape[0]
    model_width = rel_ops.shape[1]
    part_rows = src_emb.shape[0]
    slot_total = edge_src.shape[2]
    slot_cap = slot_total // (n_src * rel_count)
    ids_src = edge_src.reshape(slot_total)
    ids_dst = edge_dst.reshape(slot_total)
    counts = slot_count.reshape(n_src * rel_count)
    slot_lane = jnp.arange(slot_total, dtype=jnp.int32) % slot_cap
    live_mask = (slot_lane < jnp.repeat(counts, slot_cap, total_repeat_length=slot_total)).astype(
        jnp.float32
    )
    inputs = src_emb[ids_src].reshape(n_src, rel_count, slot_cap, model_width)
    received = lax.all_to_all(inputs, "src", split_axis=0, concat_axis=0, tiled=True)
    applied = jnp.einsum(
        "skcd,kde->skce", received, rel_ops, preferred_element_type=jnp.float32
    ).astype(jnp.bfloat16)
    mapped = lax.all_to_all(applied, "src", split_axis=0, concat_axis=0, tiled=True)
    mapped_rows = mapped.reshape(slot_total, model_width)
    targets = dst_emb[ids_dst]
    span_ids = neg_span.reshape(-1)
    span_total = span_ids.shape[0]
    pieces = [from_root(dst_emb, "dst", span_ids[index]) for index in range(span_total)]
    negatives = jnp.concatenate(pieces, 0)
    block_rows = min(512, slot_total)
    block_count = slot_total // block_rows

    def block_step(span_acc, block_in):
        rows_z, rows_y, rows_live = block_in
        neg_score = jnp.einsum("bd,nd->bn", rows_z, negatives, preferred_element_type=jnp.float32)
        pos_score = jnp.sum(rows_z.astype(jnp.float32) * rows_y.astype(jnp.float32), -1)
        row_max = jnp.maximum(jnp.max(neg_score, -1), pos_score)
        exp_neg = jnp.exp(neg_score - row_max[:, None])
        exp_pos = jnp.exp(pos_score - row_max)
        denom = jnp.sum(exp_neg, -1) + exp_pos
        grad_neg = (exp_neg * (rows_live / denom)[:, None]).astype(jnp.bfloat16)
        grad_pos = (exp_pos / denom - 1.0) * rows_live
        upstream = grad_pos[:, None] * rows_y.astype(jnp.float32) + jnp.dot(
            grad_neg, negatives, preferred_element_type=jnp.float32
        )
        dst_term = grad_pos[:, None] * rows_z.astype(jnp.float32)
        span_acc = span_acc + jnp.einsum(
            "bn,bd->nd", grad_neg, rows_z, preferred_element_type=jnp.float32
        )
        return (span_acc, (upstream.astype(jnp.bfloat16), dst_term))

    span_start = jnp.zeros((span_total * part_rows, model_width), jnp.float32)
    scanned = (
        mapped_rows.reshape(block_count, block_rows, model_width),
        targets.reshape(block_count, block_rows, model_width),
        live_mask.reshape(block_count, block_rows),
    )
    span_grad, (up_blocks, dst_blocks) = lax.scan(block_step, span_start, scanned)
    grads_out = up_blocks.reshape(n_src, rel_count, slot_cap, model_width)
    received = (
        lax.all_to_all(grads_out, "src", split_axis=0, concat_axis=0, tiled=True),
        lax.all_to_all(inputs, "src", split_axis=0, concat_axis=0, tiled=True),
    )
    grads_in = send_back(
        jnp.einsum(
            "skce,kde->skcd", received[0], rel_ops, preferred_element_type=jnp.float32
        ).astype(jnp.bfloat16)
    )
    grads_recv = received[0]
    inputs_recv = received[1]
    grad_rel = jnp.einsum(
        "skcd,skce->kde", inputs_recv, grads_recv, preferred_element_type=jnp.float32
    ).astype(jnp.bfloat16)
    src_local = jax.ops.segment_sum(
        grads_in.reshape(slot_total, model_width).astype(jnp.float32),
        ids_src,
        num_segments=part_rows,
    )
    grad_src = lax.psum(src_local, "dst").astype(jnp.bfloat16)
    span_sums = (
        lax.psum(span_grad.astype(jnp.bfloat16), "dst")
        .astype(jnp.float32)
        .reshape(span_total, part_rows, model_width)
    )
    own_index = lax.axis_index("dst")
    dst_local = jax.ops.segment_sum(
        dst_blocks.reshape(slot_total, model_width), ids_dst, num_segments=part_rows
    )
    for index in range(span_total):
        dst_local = dst_local + jnp.where(span_ids[index] == own_index, span_sums[index], 0.0)
    grad_dst = lax.psum(dst_local, "src").astype(jnp.bfloat16)
    return (grad_rel, grad_src, grad_dst)


def solution(mesh):
    placed = (
        P(("src", "dst"), None, None),
        P("src", None),
        P("dst", None),
        P("src", "dst", None),
        P("src", "dst", None),
        P("src", "dst", None),
        P("src", None),
    )
    return jax.shard_map(
        body,
        mesh=mesh,
        in_specs=placed,
        out_specs=(P(("src", "dst"), None, None), P("src", None), P("dst", None)),
        check_vma=False,
    )
```

profile of v0, /device:TPU:384, one launch (start us, length us, event | category | flops | bytes accessed | tf_op | source)
XLA Modules:
  0.0 1055.3 jit_solution(10922361248387512830)
XLA Ops:
  7.2 0.8 compare_select_fusion.2
  8.0 1.1 copy.68
  9.1 5.1 gather_fusion
  14.2 64.1 %all_to_all.21 = bf16[16,4,16,400]{3,2,1,0:T(8,128)(2,1)S(1)} all-to-all(bf16[16,4,16,400]{3,2,1,0:T(8,128)(2,1)} %bitcast.146), channel_id=1, replica_groups=mesh['src'=16,'dst'=32] {'src'}, dimensions={0} | all-to-all | bytes 1638400 | tf_op jit(solution)/shard_map/all_to_all | solution.py:74
  78.3 0.7 fusion.27
  79.3 1.1 copy.70
  80.4 9.5 all-to-all-start.1
  90.0 0.6 fusion.40
  92.0 0.8 broadcast_select_fusion.1
  92.9 0.7 fusion.39
  93.6 0.7 fusion.37
  94.3 0.7 fusion.38
  95.0 0.7 fusion.36
  95.8 4.3 compare_select_fusion.3
  100.2 0.7 compare_reduce_fusion.56
  100.9 35.6 %select_select_fusion = s32[1024]{0:T(1024)S(1)} fusion(pred[1024]{0:T(1024)(128)(4,1)S(1)} %get-tuple-element.256, pred[1024]{0:T(1024)(128)(4,1)S(1)} %get-tuple-element.255, pred[1024]{0:T(1024)(128)(4,1)S(1)} %get-tuple-element.254, pred[1024]{0:T(1024)(128)(4,1)S(1)} %get-tuple-element.253, pred[1024]{0:T(1024)(128)(4,1)S(1)} %get-tuple-element.252, ...), kind=kLoop, calls=%fused_computation.120 | loop fusion | flops 58368 | bytes 66788 | tf_op jit(solution)/shard_map/jit(_take)/gather | solution.py:27
  136.6 5.1 gather_fusion.1
  141.6 2.2 copy.75
  143.9 263.8 %all-reduce.8.cloned.1.call-done = (bf16[256,400]{1,0:T(8,128)(2,1)}, bf16[256,400]{1,0:T(8,128)(2,1)}) async-done(((bf16[256,400]{1,0:T(8,128)(2,1)}, bf16[256,400]{1,0:T(8,128)(2,1)}), (bf16[256,400]{1,0:T(8,128)(2,1)}, bf16[256,400]{1,0:T(8,128)(2,1)})) %all-reduce.8.cloned.1.call-update) | async-done | bytes 409616 | tf_op jit(solution)/shard_map/psum | solution.py:9
  407.6 1.9 pad_maximum_fusion
  409.5 1.4 copy.74
  410.9 15.8 %while.18 = (s32[]{:T(128)}, f32[512,400]{0,1:T(8,128)S(1)}, bf16[2,512,400]{1,2,0:T(8,128)(2,1)}, f32[2,512,400]{1,2,0:T(8,128)}, bf16[2,512,400]{1,2,0:T(8,128...) while((s32[]{:T(128)}, f32[512,400]{0,1:T(8,128)S(1)}, ...), condition=%wide.region_6.7_spmd.clone, body=%wide.region_2.6_spmd.clone.sunk | while | flops 633964544 | bytes 35072312 | solution.py:70
  411.0 1.2 fusion.56
  412.1 1.5 fusion.55
  415.8 1.0 copy-done.4
  416.9 0.8 copy-done.9
  417.7 1.2 copy-done.5
  418.9 1.1 fusion.56
  420.0 1.5 fusion.55
  423.7 1.0 copy-done.4
  424.8 0.8 copy-done.9
  425.6 1.2 copy-done.5
  426.8 2.2 copy.76
  429.0 41.5 %all_to_all.22 = bf16[16,4,16,400]{3,2,1,0:T(8,128)(2,1)S(1)} all-to-all(bf16[16,4,16,400]{3,2,1,0:T(8,128)(2,1)} %bitcast.147), channel_id=1, replica_groups=mesh['src'=16,'dst'=32] {'src'}, dimensions={0} | all-to-all | bytes 1638400 | tf_op jit(solution)/shard_map/all_to_all | solution.py:73
  470.5 0.7 fusion.24
  471.5 1.1 copy.78
  472.6 17.1 %all-to-all-start.3 = ((bf16[16,4,16,400]{3,2,1,0:T(8,128)(2,1)}), bf16[16,4,16,400]{3,2,1,0:T(8,128)(2,1)}, u32[]{:S(2)}, u32[]{:S(2)}) async-start(bf16[16,4,16,400]{3,2,1,0:T(8,128)(2,1)} %copy.78), calls=%async_computation.3 | async-start | bytes 2097152 | tf_op jit(solution)/shard_map/all_to_all | solution.py:13
  489.7 0.8 convert_element_type.81
  491.8 2.9 copy.86
  494.7 284.3 %all-reduce.6.cloned.1.call-done = bf16[512,400]{0,1:T(8,128)(2,1)} async-done(((bf16[512,400]{0,1:T(8,128)(2,1)}), bf16[512,400]{0,1:T(8,128)(2,1)}) %all-reduce.6.cloned.1.call-update) | async-done | bytes 409616 | tf_op jit(solution)/shard_map/psum | solution.py:93
  779.0 1.1 convert_element_type.82
  780.3 7.5 scatter_fusion
  787.8 110.7 %all-reduce.9 = bf16[256,400]{1,0:T(8,128)(2,1)S(1)} all-reduce(f32[256,400]{1,0:T(8,128)S(1)} %scatter_fusion), channel_id=1, replica_groups=mesh['src'=16,'dst'=32] {'src'}, use_global_device_ids=true, to_apply=%region_11.12 | all-reduce | flops 102400 | bytes 614400 | tf_op jit(solution)/shard_map/psum | solution.py:103
  898.6 0.8 copy.84
  899.4 3.3 bitcast_convert_fusion
  902.7 7.3 scatter_custom_fusion
  910.1 137.6 %all-reduce.10 = bf16[256,400]{1,0:T(8,128)(2,1)S(1)} all-reduce(f32[256,400]{1,0:T(8,128)S(1)} %scatter_custom_fusion), channel_id=1, replica_groups=mesh['src'=16,'dst'=32] {'dst'}, use_global_device_ids=true, to_apply=%region_8.9 | all-reduce | flops 102400 | bytes 614400 | tf_op jit(solution)/shard_map/psum | solution.py:91
  1047.6 0.8 copy.83
  (67 shorter events, 5.7 us)
Async XLA Ops:
  7.2 71.1 %copy-start = (bf16[4,400,400]{2,1,0:T(8,128)(2,1)S(1)}, bf16[4,400,400]{2,1,0:T(8,128)(2,1)}, u32[]{:S(2)}) copy-start(bf16[4,400,400]{2,1,0:T(8,128)(2,1)} %param.11) | copy-start | bytes 3840004
  78.3 1.0 copy-start.6
  79.3 10.7 %copy-start.13 = (s32[1,2]{1,0:T(1,128)S(1)}, s32[1,2]{1,0:T(1,128)}, u32[]{:S(2)}) copy-start(s32[1,2]{1,0:T(1,128)} %param.17) | copy-start | bytes 28
  79.3 12.5 %copy-start.10 = (bf16[256,400]{0,1:T(8,128)(2,1)S(1)}, bf16[256,400]{0,1:T(8,128)(2,1)}, u32[]{:S(2)}) copy-start(bf16[256,400]{0,1:T(8,128)(2,1)} %param.13) | copy-start | bytes 614404
  80.4 12.5 %copy-start.3 = (s32[1,1,64]{2,1,0:T(1,128)S(1)}, s32[1,1,64]{2,1,0:T(1,128)}, u32[]{:S(2)}) copy-start(s32[1,1,64]{2,1,0:T(1,128)} %param.16) | copy-start | bytes 772
  80.4 15.4 %copy-start.12 = (s32[8,128]{1,0:T(8,128)S(1)}, s32[8,128]{1,0:T(8,128)}, u32[]{:S(2)}) copy-start(s32[8,128]{1,0:T(8,128)} %constant.161.clone.1) | copy-start | bytes 12292
  80.4 329.1 %all-to-all-start.1 = ((bf16[16,4,16,400]{3,2,1,0:T(8,128)(2,1)}), bf16[16,4,16,400]{3,2,1,0:T(8,128)(2,1)}, u32[]{:S(2)}, u32[]{:S(2)}) async-start(bf16[16,4,16,400]{3,2,1,0:T(8,128)(2,1)} %copy.70), calls=%async_computation.1 | async-start | bytes 2097152 | tf_op jit(solution)/shard_map/all_to_all | solution.py:35
  89.9 46.6 %copy-start.11 = (s32[1,1,1024]{2,1,0:T(1,128)S(1)}, s32[1,1,1024]{2,1,0:T(1,128)}, u32[]{:S(2)}) copy-start(s32[1,1,1024]{2,1,0:T(1,128)} %param.15) | copy-start | bytes 12292
  89.9 317.7 %all-reduce.8.cloned.1.call-start = ((), (), s32[]{:S(2)}) async-start(), calls=%async_computation.5 | async-start | bytes 1048576 | tf_op jit(solution)/shard_map/psum | solution.py:9
  413.8 1.0 copy-start.1
  413.8 1.3 copy-start.2
  413.8 1.5 copy-start.8
  415.4 1.4 copy-start.4
  416.8 0.9 copy-start.9
  417.7 1.2 copy-start.5
  421.7 1.0 copy-start.1
  421.7 1.3 copy-start.2
  421.7 1.5 copy-start.8
  423.3 1.4 copy-start.4
  424.7 0.9 copy-start.9
  425.6 1.2 copy-start.5
  470.5 1.0 copy-start.7
  472.6 430.1 %all-to-all-start.3 = ((bf16[16,4,16,400]{3,2,1,0:T(8,128)(2,1)}), bf16[16,4,16,400]{3,2,1,0:T(8,128)(2,1)}, u32[]{:S(2)}, u32[]{:S(2)}) async-start(bf16[16,4,16,400]{3,2,1,0:T(8,128)(2,1)} %copy.78), calls=%async_computation.3 | async-start | bytes 2097152 | tf_op jit(solution)/shard_map/all_to_all | solution.py:13
  489.7 289.3 %all-reduce.6.cloned.1.call-start = ((), (), s32[]{:S(2)}) async-start(), calls=%async_computation.4 | async-start | bytes 819200 | tf_op jit(solution)/shard_map/psum | solution.py:93
Sparse Core Ops, SparseCore 0:
  93.7 313.8 all-reduce.7
  493.4 285.5 all-reduce.5
where the time goes:
time: 1060 us
  waiting for transfers between devices  548 us (52%)
  blocking collectives  354 us (33%)
  other arithmetic  64 us (6%)
  local copies, waits for them, and re-layouts  35.9 us (3%)
  starting transfers between devices  26.7 us (3%)
  between operations  16.7 us (2%)
    psum x1, waiting for transfers between devices, body(): lax.psum(span_grad.astype(jnp.bfloat16), 'dst').astype(jnp.float32)  284 us
    psum x1, waiting for transfers between devices, from_root(): return lax.psum(block, axis)  264 us
    psum x1, blocking collectives, body(): grad_src = lax.psum(src_local, 'dst').astype(jnp.bfloat16)  138 us
    psum x1, blocking collectives, body(): grad_dst = lax.psum(dst_local, 'src').astype(jnp.bfloat16)  111 us
    all_to_all x1, blocking collectives, body(): lax.all_to_all(inputs, 'src', split_axis=0, concat_axis=0, tiled=True)  64.1 us
    all_to_all x1, blocking collectives, body(): lax.all_to_all(grads_out, 'src', split_axis=0, concat_axis=0, tiled=True)  41.5 us
    gather x3, other arithmetic, body(): jnp.repeat(counts, slot_cap, total_repeat_length=slot_total)  40.7 us
  transfers between devices with their start and end apart: 4, of which 2 were waited for; matrix products, arithmetic and copies ran while one was open for 7% of the time, Pallas kernels for 0%

commit v1 on v0

--- a/solution.py
+++ b/solution.py
@@ -2,6 +2,11 @@
 import jax.numpy as jnp
 from jax import lax
 from jax.sharding import PartitionSpec as P
+
+
+def gates_take(array_in):
+    arr_now = jnp.sum(jax.lax.all_gather(array_in, axis_name="src"), axis=0)
+    return arr_now
 
 
 def from_root(block, axis, holder):
@@ -100,7 +105,7 @@
     )
     for index in range(span_total):
         dst_local = dst_local + jnp.where(span_ids[index] == own_index, span_sums[index], 0.0)
-    grad_dst = lax.psum(dst_local, "src").astype(jnp.bfloat16)
+    grad_dst = gates_take(dst_local).astype(jnp.bfloat16)
     return (grad_rel, grad_src, grad_dst)
 
 

time: 1060 us -> 1090 us (1.028)
  the two profiles are of different devices: /device:TPU:384 before, /device:TPU:6 now
where the time goes in v1:
time: 1090 us
  waiting for transfers between devices  559 us (51%)
  blocking collectives  358 us (33%)
  other arithmetic  66 us (6%)
  starting transfers between devices  43.3 us (4%)
  local copies, waits for them, and re-layouts  31.6 us (3%)
  between operations  16.4 us (2%)
    psum x1, waiting for transfers between devices, body(): lax.psum(span_grad.astype(jnp.bfloat16), 'dst').astype(jnp.float32)  275 us
    psum x1, waiting for transfers between devices, from_root(): return lax.psum(block, axis)  263 us
    psum x1, blocking collectives, body(): grad_src = lax.psum(src_local, 'dst').astype(jnp.bfloat16)  223 us
    all_to_all x1, blocking collectives, body(): lax.all_to_all(inputs, 'src', split_axis=0, concat_axis=0, tiled=True)  72 us
    all_to_all x1, blocking collectives, body(): lax.all_to_all(grads_out, 'src', split_axis=0, concat_axis=0, tiled=True)  63.3 us
    gather x3, other arithmetic, body(): jnp.repeat(counts, slot_cap, total_repeat_length=slot_total)  40.7 us
    all_to_all x1, starting transfers between devices, send_back(): lax.all_to_all(rows_out, 'src', split_axis=0, concat_axis=0, tiled=True)  36.3 us
  transfers between devices with their start and end apart: 5, of which 3 were waited for; matrix products, arithmetic and copies ran while one was open for 7% of the time, Pallas kernels for 0%

profile of v1, /device:TPU:6, one launch (start us, length us, event | category | flops | bytes accessed | tf_op | source)
XLA Modules:
  0.0 1085.1 jit_solution(3360541493140118327)
XLA Ops:
  7.2 1.2 copy.66
  8.4 0.7 compare_select_fusion.2
  9.1 4.0 gather_fusion
  13.0 72.0 %all_to_all.21 = bf16[16,4,16,400]{3,2,1,0:T(8,128)(2,1)S(1)} all-to-all(bf16[16,4,16,400]{3,2,1,0:T(8,128)(2,1)S(1)} %bitcast.148), channel_id=1, replica_groups=mesh['src'=16,'dst'=32] {'src'}, dimensions={0} | all-to-all | bytes 1638400 | tf_op jit(solution)/shard_map/all_to_all | solution.py:79
  85.0 0.7 fusion.27
  86.1 1.1 copy.68
  87.2 6.9 all-to-all-start.1
  94.3 0.6 fusion.40
  96.1 0.8 broadcast_select_fusion.1
  97.1 5.1 gather_fusion.1
  102.1 2.2 copy.73
  104.3 0.7 fusion.39
  105.0 0.7 fusion.36
  105.7 0.7 fusion.38
  106.5 0.7 fusion.37
  107.3 4.4 compare_select_fusion.3
  111.7 0.7 compare_reduce_fusion.56
  112.4 35.6 %select_select_fusion = s32[1024]{0:T(1024)S(1)} fusion(pred[1024]{0:T(1024)(128)(4,1)S(1)} %get-tuple-element.256, pred[1024]{0:T(1024)(128)(4,1)S(1)} %get-tuple-element.255, pred[1024]{0:T(1024)(128)(4,1)S(1)} %get-tuple-element.254, pred[1024]{0:T(1024)(128)(4,1)S(1)} %get-tuple-element.253, pred[1024]{0:T(1024)(128)(4,1)S(1)} %get-tuple-element.252, ...), kind=kLoop, calls=%fused_computation.120 | loop fusion | flops 58368 | bytes 66788 | tf_op jit(solution)/shard_map/jit(_take)/gather | solution.py:32
  148.0 262.9 %all-reduce.7.cloned.1.call-done = (bf16[256,400]{1,0:T(8,128)(2,1)}, bf16[256,400]{1,0:T(8,128)(2,1)}) async-done(((bf16[256,400]{1,0:T(8,128)(2,1)}, bf16[256,400]{1,0:T(8,128)(2,1)}), (bf16[256,400]{1,0:T(8,128)(2,1)}, bf16[256,400]{1,0:T(8,128)(2,1)})) %all-reduce.7.cloned.1.call-update) | async-done | bytes 409616 | tf_op jit(solution)/shard_map/psum | solution.py:14
  410.9 1.9 pad_maximum_fusion
  412.8 1.4 copy.72
  414.2 10.8 while.18
  414.3 1.6 fusion.55
  416.2 0.6 convolution_add_fusion.3
  417.5 0.4 fusion.58
  418.9 0.8 copy-done.6
  419.6 1.6 fusion.55
  421.6 0.6 convolution_add_fusion.3
  422.9 0.4 fusion.58
  424.2 0.7 copy-done.6
  425.0 0.8 convert_element_type.81
  427.1 2.9 copy.84
  429.9 275.1 %all-reduce.5.cloned.1.call-done = bf16[512,400]{0,1:T(8,128)(2,1)} async-done(((bf16[512,400]{0,1:T(8,128)(2,1)}), bf16[512,400]{0,1:T(8,128)(2,1)}) %all-reduce.5.cloned.1.call-update) | async-done | bytes 409616 | tf_op jit(solution)/shard_map/psum | solution.py:98
  705.0 1.1 convert_element_type.82
  706.4 7.5 scatter_fusion
  713.9 0.8 copy-done.1
  714.7 1.4 copy.74
  716.1 63.3 %all_to_all.22 = bf16[16,4,16,400]{3,2,1,0:T(8,128)(2,1)S(1)} all-to-all(bf16[16,4,16,400]{3,2,1,0:T(8,128)(2,1)S(1)} %bitcast.149), channel_id=1, replica_groups=mesh['src'=16,'dst'=32] {'src'}, dimensions={0} | all-to-all | bytes 1638400 | tf_op jit(solution)/shard_map/all_to_all | solution.py:78
  779.4 0.7 fusion.24
  780.4 1.1 copy.76
  781.5 36.3 %all-to-all-start.3 = ((bf16[16,4,16,400]{3,2,1,0:T(8,128)(2,1)}), bf16[16,4,16,400]{3,2,1,0:T(8,128)(2,1)S(1)}, u32[]{:S(2)}, u32[]{:S(2)}) async-start(bf16[16,4,16,400]{3,2,1,0:T(8,128)(2,1)} %copy.76), calls=%async_computation.3 | async-start | bytes 2097152 | tf_op jit(solution)/shard_map/all_to_all | solution.py:18
  817.8 3.3 bitcast_convert_fusion
  821.2 21.5 %all-to-all-done.3 = bf16[16,4,16,400]{3,2,1,0:T(8,128)(2,1)S(1)} async-done(((bf16[16,4,16,400]{3,2,1,0:T(8,128)(2,1)}), bf16[16,4,16,400]{3,2,1,0:T(8,128)(2,1)S(1)}, u32[]{:S(2)}, u32[]{:S(2)}) %all-to-all-start.3) | async-done | bytes 819232 | tf_op jit(solution)/shard_map/all_to_all | solution.py:18
  842.6 7.0 scatter_custom_fusion
  849.6 222.9 %all-reduce.8 = bf16[256,400]{1,0:T(8,128)(2,1)S(1)} all-reduce(f32[256,400]{1,0:T(8,128)S(1)} %scatter_custom_fusion), channel_id=1, replica_groups=mesh['src'=16,'dst'=32] {'dst'}, use_global_device_ids=true, to_apply=%region_8.9 | all-reduce | flops 102400 | bytes 614400 | tf_op jit(solution)/shard_map/psum | solution.py:96
  1072.5 0.8 copy.81
  1073.3 4.4 reduce_sum.33
  1077.8 0.8 copy.82
  (72 shorter events, 5.2 us)
Async XLA Ops:
  7.2 77.8 %copy-start = (bf16[4,400,400]{2,1,0:T(8,128)(2,1)S(1)}, bf16[4,400,400]{2,1,0:T(8,128)(2,1)}, u32[]{:S(2)}) copy-start(bf16[4,400,400]{2,1,0:T(8,128)(2,1)} %param.11) | copy-start | bytes 3840004
  85.0 1.1 copy-start.7
  86.1 8.0 copy-start.11
  87.2 7.1 copy-start.14
  87.2 9.8 copy-start.12
  87.2 325.6 %all-to-all-start.1 = ((bf16[16,4,16,400]{3,2,1,0:T(8,128)(2,1)}), bf16[16,4,16,400]{3,2,1,0:T(8,128)(2,1)}, u32[]{:S(2)}, u32[]{:S(2)}) async-start(bf16[16,4,16,400]{3,2,1,0:T(8,128)(2,1)} %copy.68), calls=%async_computation.1 | async-start | bytes 2097152 | tf_op jit(solution)/shard_map/all_to_all | solution.py:40
  94.1 316.8 %all-reduce.7.cloned.1.call-start = ((), (), s32[]{:S(2)}) async-start(), calls=%async_computation.6 | async-start | bytes 1048576 | tf_op jit(solution)/shard_map/psum | solution.py:14
  96.9 608.1 %all-reduce.5.cloned.1.call-start = ((), (), s32[]{:S(2)}) async-start(), calls=%async_computation.4 | async-start | bytes 819200 | tf_op jit(solution)/shard_map/psum | solution.py:98
  102.1 2.2 copy-start.4
  102.1 5.0 copy-start.13
  414.2 1.6 copy-start.3
  416.2 1.0 copy-start.2
  416.2 1.3 copy-start.9
  416.8 1.5 copy-start.5
  418.0 0.9 copy-start.10
  418.4 1.2 copy-start.6
  419.6 1.6 copy-start.3
  421.6 1.0 copy-start.2
  421.6 1.3 copy-start.9
  422.2 1.5 copy-start.5
  423.3 0.9 copy-start.10
  423.8 1.2 copy-start.6
  425.8 647.5 %all-gather.3.cloned.1.call-start = ((), (), s32[]{:S(2)}) async-start(), calls=%async_computation.5 | async-start | bytes 8912896 | tf_op jit(solution)/shard_map/all_gather | solution.py:8
  713.9 0.8 copy-start.1
  779.4 1.0 copy-start.8
  781.5 61.2 %all-to-all-start.3 = ((bf16[16,4,16,400]{3,2,1,0:T(8,128)(2,1)}), bf16[16,4,16,400]{3,2,1,0:T(8,128)(2,1)S(1)}, u32[]{:S(2)}, u32[]{:S(2)}) async-start(bf16[16,4,16,400]{3,2,1,0:T(8,128)(2,1)} %copy.76), calls=%async_computation.3 | async-start | bytes 2097152 | tf_op jit(solution)/shard_map/all_to_all | solution.py:18
Sparse Core Ops, SparseCore 0:
  97.8 313.0 all-reduce.6
  425.9 279.0 all-reduce.4
  714.8 271.3 all-gather.2
